TPU v7x, 128 devices: a whole 4x4x4 slice. The times are simulated.
128 devices in a mesh: gx: 16 (over z, x), gy: 8 (over y, core).
Axes of the slice: x: 4, y: 4, z: 4, core: 2. Of those that a mesh axis runs over, the one named last changes fastest.
Arguments:
- tokens: bfloat16 [2048, 8192], P('gy', 'gx'), may hold values from -6 to 6
- gate_base_weight: bfloat16 [8192, 29568], P('gx', 'gy'), may hold values from -0.0625 to 0.0625
- up_base_weight: bfloat16 [8192, 29568], P('gx', 'gy'), may hold values from -0.0625 to 0.0625
- adapter_down_maps: bfloat16 [128, 8192, 128], P(('gx', 'gy')), may hold values from -0.0625 to 0.0625
- adapter_up_maps: bfloat16 [128, 128, 29568], P(('gx', 'gy')), may hold values from -0.75 to 0.75
- tenant: int32 [2048, 1], replicated, may hold values from 0 to 127; in each aligned block of 128 rows (0 to 127, 128 to 255, ...) at most 4 rows name the same one
- tenant_slot_index: int32 [128], replicated, may hold values from 0 to 127, as said below
Outputs:
- hidden: bfloat16 [2048, 29568], P('gx', 'gy')
Inputs may be any that keep to these rules, and one draw needn't show every extreme that they name: In each aligned block of 128 rows no tenant names more than 4 rows, and in some block a tenant names exactly 4. `tenant_slot_index`: A permutation of the slots; slot s is held by device s of gx+gy, gx the slower index.
All inputs are finite; a program needn't handle non-finite values.
Results may differ from a plain program's by a relative error of at most 0.019.
Values may be sent and summed in bfloat16 or wider, within the bound.
No kernel may reach another device: no remote copies, remote signals or barrier semaphores. Data moves between devices by JAX's collectives and lax.ppermute only.
A program may use at most 192 MiB of HBM per device.

v0:
```python
import jax
import jax.numpy as jnp
from jax import lax
from jax.sharding import PartitionSpec as P

CAP = 4


def body(
    tokens,
    gate_base_weight,
    up_base_weight,
    adapter_down_maps,
    adapter_up_maps,
    tenant,
    tenant_slot_index,
):
    tile_grid_rows = lax.axis_size("gx")
    tile_grid_columns = lax.axis_size("gy")
    devices = tile_grid_rows * tile_grid_columns
    row_gx = lax.axis_index("gx")
    row_gy = lax.axis_index("gy")
    local_rows = tokens.shape[0]
    tile_width = tokens.shape[1]
    total_rows = tenant.shape[0]
    block = total_rows // tile_grid_rows
    groups = local_rows // block
    tenants = tenant_slot_index.shape[0]
    column_count = gate_base_weight.shape[1]
    doubled_rank = adapter_down_maps.shape[2]
    adapter_rank_width = doubled_rank // 2
    gathered = lax.all_gather(tokens, "gy", axis=0, tiled=True)
    summed = lax.psum_scatter(
        jnp.concatenate(
            [
                jnp.dot(gathered, gate_base_weight, preferred_element_type=jnp.float32),
                jnp.dot(gathered, up_base_weight, preferred_element_type=jnp.float32),
            ],
            axis=1,
        ).astype(jnp.bfloat16),
        "gx",
        scatter_dimension=0,
        tiled=True,
    ).astype(jnp.float32)
    slot_all = jnp.sum(
        jnp.where(tenant == lax.iota(jnp.int32, tenants)[None, :], tenant_slot_index[None, :], 0),
        axis=1,
    )
    onehot = (slot_all[:, None] == lax.iota(jnp.int32, devices)[None, :]).astype(jnp.int32)
    blocked = onehot.reshape(tile_grid_rows, block, devices)
    before = jnp.cumsum(blocked, axis=1) - blocked
    position = jnp.sum(before * blocked, axis=2).reshape(total_rows)
    send_slot = lax.dynamic_slice_in_dim(slot_all, row_gy * local_rows, local_rows)
    send_rank = lax.dynamic_slice_in_dim(position, row_gy * local_rows, local_rows)
    target = (send_slot * groups + lax.iota(jnp.int32, local_rows) // block) * CAP + send_rank
    outgoing = jnp.zeros((devices * groups * CAP, tile_width), jnp.bfloat16).at[target].set(tokens)
    arrived = lax.all_to_all(
        outgoing.reshape(devices, groups * CAP, tile_width),
        ("gx", "gy"),
        split_axis=0,
        concat_axis=0,
        tiled=True,
    )
    arrived = arrived.reshape(tile_grid_rows, tile_grid_columns * groups * CAP, tile_width)
    down_local = adapter_down_maps[0].reshape(tile_grid_rows, tile_width, doubled_rank)
    low = jnp.einsum("isk,ikr->sr", arrived, down_local, preferred_element_type=jnp.float32).astype(
        jnp.bfloat16
    )
    low = low.reshape(tile_grid_rows, CAP, doubled_rank)
    gate_up_map = adapter_up_maps[0, :adapter_rank_width].reshape(
        adapter_rank_width, tile_grid_columns, column_count
    )
    up_up_map = adapter_up_maps[0, adapter_rank_width:].reshape(
        adapter_rank_width, tile_grid_columns, column_count
    )
    delta_gate = jnp.einsum(
        "gcr,rjf->gjcf",
        low[:, :, :adapter_rank_width],
        gate_up_map,
        preferred_element_type=jnp.float32,
    ).astype(jnp.bfloat16)
    delta_up = jnp.einsum(
        "gcr,rjf->gjcf",
        low[:, :, adapter_rank_width:],
        up_up_map,
        preferred_element_type=jnp.float32,
    ).astype(jnp.bfloat16)
    back_gate, back_up = (
        lax.all_to_all(
            delta_gate.reshape(devices, CAP, column_count),
            ("gx", "gy"),
            split_axis=0,
            concat_axis=0,
            tiled=True,
        ),
        lax.all_to_all(
            delta_up.reshape(devices, CAP, column_count),
            ("gx", "gy"),
            split_axis=0,
            concat_axis=0,
            tiled=True,
        ),
    )
    back_gate = back_gate.reshape(devices * CAP, column_count)
    back_up = back_up.reshape(devices * CAP, column_count)
    own_slot = lax.dynamic_slice_in_dim(slot_all, row_gx * block, block)
    own_rank = lax.dynamic_slice_in_dim(position, row_gx * block, block)
    pick = own_slot * CAP + own_rank
    gate_value = summed[:, :column_count] + back_gate[pick].astype(jnp.float32)
    up_value = summed[:, column_count:] + back_up[pick].astype(jnp.float32)
    return (jax.nn.silu(gate_value) * up_value).astype(jnp.bfloat16)


def solution(mesh):
    return jax.shard_map(
        body,
        mesh=mesh,
        in_specs=(
            P("gy", "gx"),
            P("gx", "gy"),
            P("gx", "gy"),
            P(("gx", "gy"), None, None),
            P(("gx", "gy"), None, None),
            P(),
            P(),
        ),
        out_specs=P("gx", "gy"),
        check_vma=False,
    )
```

profile of v0, /device:TPU:1, one launch (start us, length us, event | category | flops | bytes accessed | tf_op | source)
XLA Modules:
  0.0 404.3 jit_solution(10806545864353587675)
XLA Ops:
  7.3 30.6 %all-gather.2.cloned.1.call-done = bf16[2048,512]{1,0:T(8,128)(2,1)} async-done(((bf16[256,512]{1,0:T(8,128)(2,1)}), bf16[2048,512]{1,0:T(8,128)(2,1)}) %all-gather.2.cloned.1.call-update) | async-done | bytes 2097168 | tf_op jit(solution)/shard_map/all_gather | solution.py:32
  37.9 13.8 %convolution_convert_fusion = bf16[2048,3696]{0,1:T(8,128)(2,1)} fusion(bf16[2048,512]{1,0:T(8,128)(2,1)} %all-gather.2.cloned.1.call-done, bf16[512,3696]{0,1:T(8,128)(2,1)} %param.9), kind=kOutput, calls=%fused_computation.4 | convolution fusion | flops 7758643200 | bytes 21020672 | tf_op jit(solution)/shard_map/dot_general | solution.py:37
  51.8 10.8 %convolution_convert_fusion.1 = bf16[2048,3696]{0,1:T(8,128)(2,1)} fusion(bf16[2048,512]{1,0:T(8,128)(2,1)S(1)} %copy-done.6, bf16[512,3696]{0,1:T(8,128)(2,1)S(1)} %copy-done.5), kind=kOutput, calls=%fused_computation.5 | convolution fusion | flops 7758643200 | bytes 21020672 | tf_op jit(solution)/shard_map/dot_general | solution.py:36
  62.6 21.4 %pad_maximum_fusion = bf16[2048,7392]{0,1:T(8,128)(2,1)} fusion(bf16[2048,3696]{0,1:T(8,128)(2,1)} %convolution_convert_fusion, bf16[2048,3696]{0,1:T(8,128)(2,1)} %convolution_convert_fusion.1), kind=kLoop, calls=%fused_computation.3 | loop fusion | flops 60555264 | bytes 60555264 | tf_op jit(solution)/shard_map/concatenate | solution.py:34
  84.0 36.5 %copy.60 = bf16[2048,7392]{1,0:T(8,128)(2,1)} copy(bf16[2048,7392]{0,1:T(8,128)(2,1)} %pad_maximum_fusion) | data formatting | bytes 60555264
  124.9 3.1 scatter_custom_fusion
  127.9 8.1 %all-to-all-start = ((bf16[128,8,512]{2,1,0:T(8,128)(2,1)}), bf16[128,8,512]{2,1,0:T(8,128)(2,1)S(1)}, u32[]{:S(2)}, u32[]{:S(2)}) async-start(bf16[128,8,512]{2,1,0:T(8,128)(2,1)} %bitcast.48), calls=%async_computation | async-start | bytes 2097152 | tf_op jit(solution)/shard_map/all_to_all | solution.py:57
  136.1 5.6 %fusion.19 = (bf16[1,64,29568]{2,1,0:T(8,128)(2,1)}, bf16[1,64,29568]{2,1,0:T(8,128)(2,1)}) fusion(bf16[1,128,29568]{2,1,0:T(8,128)(2,1)} %param.11), kind=kLoop, calls=%fused_computation.44 | loop fusion | bytes 15138816 | tf_op jit(solution)/shard_map/slice | solution.py:70
  141.7 7.5 %reshape_squeeze.11 = bf16[64,8,3696]{2,1,0:T(8,128)(2,1)} reshape(bf16[1,64,29568]{2,1,0:T(8,128)(2,1)} %get-tuple-element.6) | data formatting | bytes 7569408 | tf_op jit(solution)/shard_map/reshape;squeeze | solution.py:73
  149.2 17.1 %all-to-all-done = bf16[128,8,512]{2,1,0:T(8,128)(2,1)S(1)} async-done(((bf16[128,8,512]{2,1,0:T(8,128)(2,1)}), bf16[128,8,512]{2,1,0:T(8,128)(2,1)S(1)}, u32[]{:S(2)}, u32[]{:S(2)}) %all-to-all-start) | async-done | bytes 1048608 | tf_op jit(solution)/shard_map/all_to_all | solution.py:57
  166.9 3.3 fusion.1
  170.9 4.9 %copy.56 = bf16[128,4,3696]{2,1,0:T(4,128)(2,1)} copy(bf16[128,4,3696]{2,0,1:T(8,128)(2,1)S(1)} %bitcast.45) | data formatting | bytes 7569408 | tf_op jit(solution)/shard_map/reshape | solution.py:97
  175.8 6.1 %all-to-all-start.2 = ((bf16[128,4,3696]{2,1,0:T(4,128)(2,1)}), bf16[128,4,3696]{2,1,0:T(4,128)(2,1)}, u32[]{:S(2)}, u32[]{:S(2)}) async-start(bf16[128,4,3696]{2,1,0:T(4,128)(2,1)} %copy.56), calls=%async_computation.2 | async-start | bytes 7602176 | tf_op jit(solution)/shard_map/all_to_all | solution.py:96
  181.9 7.5 %reshape_squeeze.10 = bf16[64,8,3696]{2,1,0:T(8,128)(2,1)} reshape(bf16[1,64,29568]{2,1,0:T(8,128)(2,1)} %get-tuple-element.5) | data formatting | bytes 7569408 | tf_op jit(solution)/shard_map/reshape;squeeze | solution.py:70
  189.4 3.2 fusion
  193.3 4.8 %copy.52 = bf16[128,4,3696]{2,1,0:T(4,128)(2,1)} copy(bf16[128,4,3696]{2,0,1:T(8,128)(2,1)S(1)} %bitcast.46) | data formatting | bytes 7569408 | tf_op jit(solution)/shard_map/reshape | solution.py:90
  198.0 65.6 %all-to-all-done.2 = bf16[128,4,3696]{2,1,0:T(4,128)(2,1)} async-done(((bf16[128,4,3696]{2,1,0:T(4,128)(2,1)}), bf16[128,4,3696]{2,1,0:T(4,128)(2,1)}, u32[]{:S(2)}, u32[]{:S(2)}) %all-to-all-start.2) | async-done | bytes 3784736 | tf_op jit(solution)/shard_map/all_to_all | solution.py:96
  263.6 6.3 %all-to-all-start.1 = ((bf16[128,4,3696]{2,1,0:T(4,128)(2,1)}), bf16[128,4,3696]{2,1,0:T(4,128)(2,1)}, u32[]{:S(2)}, u32[]{:S(2)}) async-start(bf16[128,4,3696]{2,1,0:T(4,128)(2,1)} %copy.52), calls=%async_computation.1 | async-start | bytes 7602176 | tf_op jit(solution)/shard_map/all_to_all | solution.py:89
  270.0 7.2 %reshape.42 = bf16[512,3696]{1,0:T(8,128)(2,1)} reshape(bf16[128,4,3696]{2,1,0:T(4,128)(2,1)} %all-to-all-done.2) | data formatting | bytes 7569408 | tf_op jit(solution)/shard_map/reshape | solution.py:105
  277.2 5.8 %gather_fusion.1 = bf16[128,3696]{1,0:T(8,128)(2,1)} fusion(bf16[512,3696]{1,0:T(8,128)(2,1)} %reshape.42, s32[1024]{0:T(1024)S(1)} %pad_clamp_fusion), kind=kCustom, calls=%fused_computation.1 | custom fusion | bytes 1892864 | tf_op jit(solution)/shard_map/gather | solution.py:110
  283.0 68.3 %all-to-all-done.1 = bf16[128,4,3696]{2,1,0:T(4,128)(2,1)} async-done(((bf16[128,4,3696]{2,1,0:T(4,128)(2,1)}), bf16[128,4,3696]{2,1,0:T(4,128)(2,1)}, u32[]{:S(2)}, u32[]{:S(2)}) %all-to-all-start.1) | async-done | bytes 3784736 | tf_op jit(solution)/shard_map/all_to_all | solution.py:89
  351.3 7.0 %reshape.40 = bf16[512,3696]{1,0:T(8,128)(2,1)} reshape(bf16[128,4,3696]{2,1,0:T(4,128)(2,1)} %all-to-all-done.1) | data formatting | bytes 7569408 | tf_op jit(solution)/shard_map/reshape | solution.py:104
  358.3 5.9 %gather_fusion = bf16[128,3696]{1,0:T(8,128)(2,1)} fusion(bf16[512,3696]{1,0:T(8,128)(2,1)} %reshape.40, s32[1024]{0:T(1024)S(1)} %pad_clamp_fusion), kind=kCustom, calls=%fused_computation | custom fusion | bytes 1892864 | tf_op jit(solution)/shard_map/gather | solution.py:109
  364.2 29.1 %reduce-scatter.4.cloned.1.call-done = bf16[128,7392]{1,0:T(8,128)(2,1)} async-done(((bf16[2048,7392]{1,0:T(8,128)(2,1)}), bf16[128,7392]{1,0:T(8,128)(2,1)}) %reduce-scatter.4.cloned.1.call-update) | async-done | bytes 1892368 | tf_op jit(solution)/shard_map/reduce_scatter | solution.py:33
  (32 shorter events, 11.3 us)
Async XLA Ops:
  6.5 159.8 %copy-start = (bf16[1,8192,128]{2,1,0:T(8,128)(2,1)S(1)}, bf16[1,8192,128]{2,1,0:T(8,128)(2,1)}, u32[]{:S(2)}) copy-start(bf16[1,8192,128]{2,1,0:T(8,128)(2,1)} %param.10) | copy-start | bytes 6291460
  6.5 31.4 %all-gather.2.cloned.1.call-start = ((), (), s32[]{:S(2)}) async-start(), calls=%async_computation.4 | async-start | bytes 2359296 | tf_op jit(solution)/shard_map/all_gather | solution.py:32
  7.3 386.0 %reduce-scatter.4.cloned.1.call-start = ((), (), s32[]{:S(2)}) async-start(), calls=%async_computation.5 | async-start | bytes 32309248 | tf_op jit(solution)/shard_map/reduce_scatter | solution.py:33
  37.9 13.8 %copy-start.5 = (bf16[512,3696]{0,1:T(8,128)(2,1)S(1)}, bf16[512,3696]{0,1:T(8,128)(2,1)}, u32[]{:S(2)}) copy-start(bf16[512,3696]{0,1:T(8,128)(2,1)} %param.8) | copy-start | bytes 11354116
  37.9 13.8 %copy-start.6 = (bf16[2048,512]{1,0:T(8,128)(2,1)S(1)}, bf16[2048,512]{1,0:T(8,128)(2,1)}, u32[]{:S(2)}) copy-start(bf16[2048,512]{1,0:T(8,128)(2,1)} %all-gather.2.cloned.1.call-done) | copy-start | bytes 6291460
  120.5 0.7 copy-start.3
  120.5 0.7 copy-start.4
  127.9 38.4 %all-to-all-start = ((bf16[128,8,512]{2,1,0:T(8,128)(2,1)}), bf16[128,8,512]{2,1,0:T(8,128)(2,1)S(1)}, u32[]{:S(2)}, u32[]{:S(2)}) async-start(bf16[128,8,512]{2,1,0:T(8,128)(2,1)} %bitcast.48), calls=%async_computation | async-start | bytes 2097152 | tf_op jit(solution)/shard_map/all_to_all | solution.py:57
  175.8 87.8 %all-to-all-start.2 = ((bf16[128,4,3696]{2,1,0:T(4,128)(2,1)}), bf16[128,4,3696]{2,1,0:T(4,128)(2,1)}, u32[]{:S(2)}, u32[]{:S(2)}) async-start(bf16[128,4,3696]{2,1,0:T(4,128)(2,1)} %copy.56), calls=%async_computation.2 | async-start | bytes 7602176 | tf_op jit(solution)/shard_map/all_to_all | solution.py:96
  263.6 87.7 %all-to-all-start.1 = ((bf16[128,4,3696]{2,1,0:T(4,128)(2,1)}), bf16[128,4,3696]{2,1,0:T(4,128)(2,1)}, u32[]{:S(2)}, u32[]{:S(2)}) async-start(bf16[128,4,3696]{2,1,0:T(4,128)(2,1)} %copy.52), calls=%async_computation.1 | async-start | bytes 7602176 | tf_op jit(solution)/shard_map/all_to_all | solution.py:89
  393.3 1.9 copy-start.1
  393.3 2.0 copy-start.2
Sparse Core Ops, SparseCore 0:
  9.1 28.7 all-gather.1
  120.6 272.5 reduce-scatter.3
where the time goes:
time: 406 us; the launch traced here: 404 us
  waiting for transfers between devices  211 us (52%)
  local copies, waits for them, and re-layouts  99.4 us (24%)
  matrix products  31.7 us (8%)
  other arithmetic  27.8 us (7%)
  starting transfers between devices  20.6 us (5%)
  between operations  13.5 us (3%)
    all_to_all x1, waiting for transfers between devices, body(): lax.all_to_all(delta_gate.reshape(devices, CAP, column_count), ('gx', 'gy...  68.3 us
    all_to_all x1, waiting for transfers between devices, body(): lax.all_to_all(delta_up.reshape(devices, CAP, column_count), ('gx', 'gy')...  65.6 us
    unnamed x15, local copies, waits for them, and re-layouts  37.3 us
    all_gather x1, waiting for transfers between devices, body(): gathered = lax.all_gather(tokens, 'gy', axis=0, tiled=True)  30.6 us
    reduce_scatter x1, waiting for transfers between devices, body(): lax.psum_scatter(jnp.concatenate([jnp.dot(gathered, gate_base_weight, pre...  29.1 us
    concatenate x1, other arithmetic, body(): jnp.concatenate([jnp.dot(gathered, gate_base_weight, preferred_element_ty...  21.4 us
    all_to_all x1, waiting for transfers between devices, body(): lax.all_to_all(outgoing.reshape(devices, groups * CAP, tile_width), ('gx'...  17.1 us
    dot_general x1, matrix products, body(): jnp.dot(gathered, up_base_weight, preferred_element_type=jnp.float32)  13.8 us
  transfers between devices with their start and end apart: 5, of which 5 were waited for; matrix products, arithmetic and copies ran while one was open for 18% of the time, Pallas kernels for 0%

commit v1 on v0

--- a/solution.py
+++ b/solution.py
@@ -4,6 +4,19 @@
 from jax.sharding import PartitionSpec as P
 
 CAP = 4
+
+
+def collect(value, axis, dim):
+    ways = lax.axis_size(axis)
+    up = [(d, (d + 1) % ways) for d in range(ways)]
+    down = [(d, (d - 1) % ways) for d in range(ways)]
+    earlier, later = ([value], [value])
+    for _ in range(ways // 2):
+        earlier.append(lax.ppermute(earlier[-1], axis, up))
+    for _ in range((ways - 1) // 2):
+        later.append(lax.ppermute(later[-1], axis, down))
+    line = jnp.concatenate([*earlier[::-1], *later[1:]], axis=dim)
+    return jnp.roll(line, (lax.axis_index(axis) - ways // 2) * value.shape[dim], axis=dim)
 
 
 def body(
@@ -29,7 +42,7 @@
     column_count = gate_base_weight.shape[1]
     doubled_rank = adapter_down_maps.shape[2]
     adapter_rank_width = doubled_rank // 2
-    gathered = lax.all_gather(tokens, "gy", axis=0, tiled=True)
+    gathered = collect(tokens, "gy", 0)
     summed = lax.psum_scatter(
         jnp.concatenate(
             [

time: 406 us -> 407 us (level)
  waiting for transfers between devices: 211 us -> 192 us
  starting transfers between devices: 20.6 us -> 38.8 us
  local copies, waits for them, and re-layouts: 99.4 us -> 104 us
    all_gather x1 -> x0, waiting for transfers between devices: 30.6 us -> none  [body(): gathered = lax.all_gather(tokens, 'gy', axis=0, tiled=True)]
    ppermute x0 -> x7, starting transfers between devices: none -> 12.5 us  [the longest x4 10.1 us: collect(): earlier.append(lax.ppermute(earlier[-1], axis, up))]
    ppermute x0 -> x7, waiting for transfers between devices: none -> 11.8 us  [the longest x4 10.3 us: collect(): earlier.append(lax.ppermute(earlier[-1], axis, up))]
    all_to_all x1, starting transfers between devices: 8.15 us -> 13.2 us  [body(): lax.all_to_all(outgoing.reshape(devices, groups * CAP, tile_width), ('gx'...]
    unnamed x15 -> x32, local copies, waits for them, and re-layouts: 37.3 us -> 42.3 us
  transfers between devices with their start and end apart: 5 -> 11, of which waited for: 5 -> 11; matrix products, arithmetic and copies ran while one was open for 18% -> 18% of each run, Pallas kernels for 0% -> 0%
where the time goes in v1:
time: 407 us; the launch traced here: 404 us
  waiting for transfers between devices  192 us (47%)
  local copies, waits for them, and re-layouts  104 us (26%)
  starting transfers between devices  38.8 us (10%)
  matrix products  28.6 us (7%)
  other arithmetic  27.8 us (7%)
  between operations  13.6 us (3%)
    all_to_all x1, waiting for transfers between devices, body(): lax.all_to_all(delta_up.reshape(devices, CAP, column_count), ('gx', 'gy')...  68.8 us
    all_to_all x1, waiting for transfers between devices, body(): lax.all_to_all(delta_gate.reshape(devices, CAP, column_count), ('gx', 'gy...  65 us
    unnamed x32, local copies, waits for them, and re-layouts  42.3 us
    reduce_scatter x1, waiting for transfers between devices, body(): lax.psum_scatter(jnp.concatenate([jnp.dot(gathered, gate_base_weight, pre...  29.1 us
    concatenate x1, other arithmetic, body(): jnp.concatenate([jnp.dot(gathered, gate_base_weight, preferred_element_ty...  21.4 us
    all_to_all x1, waiting for transfers between devices, body(): lax.all_to_all(outgoing.reshape(devices, groups * CAP, tile_width), ('gx'...  17.2 us
    all_to_all x1, starting transfers between devices, body(): lax.all_to_all(outgoing.reshape(devices, groups * CAP, tile_width), ('gx'...  13.2 us
    dot_general x1, matrix products, body(): jnp.dot(gathered, gate_base_weight, preferred_element_type=jnp.float32)  10.8 us
  transfers between devices with their start and end apart: 11, of which 11 were waited for; matrix products, arithmetic and copies ran while one was open for 18% of the time, Pallas kernels for 0%

profile of v1, /device:TPU:1, one launch (start us, length us, event | category | flops | bytes accessed | tf_op | source)
XLA Modules:
  0.0 404.5 jit_solution(10574524386551290324)
XLA Ops:
  9.2 3.6 collective-permute-done
  15.2 3.3 collective-permute-done.1
  36.1 10.8 %convolution_convert_fusion.1 = bf16[2048,3696]{0,1:T(8,128)(2,1)} fusion(bf16[512,3696]{0,1:T(8,128)(2,1)S(1)} %copy-done.6, bf16[4096,512]{1,0:T(8,128)(2,1)S(1)} %constant_dynamic-update-slice_fusion, s32[]{:T(128)S(6)} %select_n.38), kind=kOutput, calls=%fused_computation.5 | convolution fusion | flops 7758643200 | bytes 21020676 | tf_op jit(solution)/shard_map/dot_general | solution.py:49
  46.9 10.8 %convolution_convert_fusion = bf16[2048,3696]{0,1:T(8,128)(2,1)} fusion(bf16[512,3696]{0,1:T(8,128)(2,1)S(1)} %copy-done.7, bf16[4096,512]{1,0:T(8,128)(2,1)S(1)} %constant_dynamic-update-slice_fusion, s32[]{:T(128)S(6)} %select_n.38), kind=kOutput, calls=%fused_computation.4 | convolution fusion | flops 7758643200 | bytes 21020676 | tf_op jit(solution)/shard_map/dot_general | solution.py:50
  57.7 21.4 %pad_maximum_fusion = bf16[2048,7392]{0,1:T(8,128)(2,1)} fusion(bf16[2048,3696]{0,1:T(8,128)(2,1)} %convolution_convert_fusion, bf16[2048,3696]{0,1:T(8,128)(2,1)} %convolution_convert_fusion.1), kind=kLoop, calls=%fused_computation.3 | loop fusion | flops 60555264 | bytes 60555264 | tf_op jit(solution)/shard_map/concatenate | solution.py:47
  79.2 36.4 %copy.60 = bf16[2048,7392]{1,0:T(8,128)(2,1)} copy(bf16[2048,7392]{0,1:T(8,128)(2,1)} %pad_maximum_fusion) | data formatting | bytes 60555264
  122.6 13.2 %all-to-all-start = ((bf16[128,8,512]{2,1,0:T(8,128)(2,1)}), bf16[128,8,512]{2,1,0:T(8,128)(2,1)S(1)}, u32[]{:S(2)}, u32[]{:S(2)}) async-start(bf16[128,8,512]{2,1,0:T(8,128)(2,1)} %bitcast.46), calls=%async_computation | async-start | bytes 2097152 | tf_op jit(solution)/shard_map/all_to_all | solution.py:70
  135.8 5.5 %fusion.23 = (bf16[1,64,29568]{2,1,0:T(8,128)(2,1)}, bf16[1,64,29568]{2,1,0:T(8,128)(2,1)}) fusion(bf16[1,128,29568]{2,1,0:T(8,128)(2,1)} %param.11), kind=kLoop, calls=%fused_computation.64 | loop fusion | bytes 15138816 | tf_op jit(solution)/shard_map/slice | solution.py:83
  141.3 7.5 %reshape_squeeze.10 = bf16[64,8,3696]{2,1,0:T(8,128)(2,1)} reshape(bf16[1,64,29568]{2,1,0:T(8,128)(2,1)} %get-tuple-element.5) | data formatting | bytes 7569408 | tf_op jit(solution)/shard_map/reshape;squeeze | solution.py:83
  148.8 17.2 %all-to-all-done = bf16[128,8,512]{2,1,0:T(8,128)(2,1)S(1)} async-done(((bf16[128,8,512]{2,1,0:T(8,128)(2,1)}), bf16[128,8,512]{2,1,0:T(8,128)(2,1)S(1)}, u32[]{:S(2)}, u32[]{:S(2)}) %all-to-all-start) | async-done | bytes 1048608 | tf_op jit(solution)/shard_map/all_to_all | solution.py:70
  166.6 3.2 fusion
  170.5 4.9 %copy.52 = bf16[128,4,3696]{2,1,0:T(4,128)(2,1)} copy(bf16[128,4,3696]{2,0,1:T(8,128)(2,1)S(1)} %bitcast.43) | data formatting | bytes 7569408 | tf_op jit(solution)/shard_map/reshape | solution.py:103
  175.4 5.9 %all-to-all-start.1 = ((bf16[128,4,3696]{2,1,0:T(4,128)(2,1)}), bf16[128,4,3696]{2,1,0:T(4,128)(2,1)}, u32[]{:S(2)}, u32[]{:S(2)}) async-start(bf16[128,4,3696]{2,1,0:T(4,128)(2,1)} %copy.52), calls=%async_computation.1 | async-start | bytes 7602176 | tf_op jit(solution)/shard_map/all_to_all | solution.py:102
  181.3 7.6 %reshape_squeeze.11 = bf16[64,8,3696]{2,1,0:T(8,128)(2,1)} reshape(bf16[1,64,29568]{2,1,0:T(8,128)(2,1)} %get-tuple-element.6) | data formatting | bytes 7569408 | tf_op jit(solution)/shard_map/reshape;squeeze | solution.py:86
  188.9 3.2 fusion.1
  192.7 4.8 %copy.56 = bf16[128,4,3696]{2,1,0:T(4,128)(2,1)} copy(bf16[128,4,3696]{2,0,1:T(8,128)(2,1)S(1)} %bitcast.44) | data formatting | bytes 7569408 | tf_op jit(solution)/shard_map/reshape | solution.py:110
  197.5 65.0 %all-to-all-done.1 = bf16[128,4,3696]{2,1,0:T(4,128)(2,1)} async-done(((bf16[128,4,3696]{2,1,0:T(4,128)(2,1)}), bf16[128,4,3696]{2,1,0:T(4,128)(2,1)}, u32[]{:S(2)}, u32[]{:S(2)}) %all-to-all-start.1) | async-done | bytes 3784736 | tf_op jit(solution)/shard_map/all_to_all | solution.py:102
  262.5 7.2 %all-to-all-start.2 = ((bf16[128,4,3696]{2,1,0:T(4,128)(2,1)}), bf16[128,4,3696]{2,1,0:T(4,128)(2,1)}, u32[]{:S(2)}, u32[]{:S(2)}) async-start(bf16[128,4,3696]{2,1,0:T(4,128)(2,1)} %copy.56), calls=%async_computation.2 | async-start | bytes 7602176 | tf_op jit(solution)/shard_map/all_to_all | solution.py:109
  269.8 7.2 %reshape.40 = bf16[512,3696]{1,0:T(8,128)(2,1)} reshape(bf16[128,4,3696]{2,1,0:T(4,128)(2,1)} %all-to-all-done.1) | data formatting | bytes 7569408 | tf_op jit(solution)/shard_map/reshape | solution.py:117
  276.9 5.6 %gather_fusion = bf16[128,3696]{1,0:T(8,128)(2,1)} fusion(bf16[512,3696]{1,0:T(8,128)(2,1)} %reshape.40, s32[1024]{0:T(1024)S(1)} %pad_clamp_fusion), kind=kCustom, calls=%fused_computation | custom fusion | bytes 1892864 | tf_op jit(solution)/shard_map/gather | solution.py:122
  282.5 68.8 %all-to-all-done.2 = bf16[128,4,3696]{2,1,0:T(4,128)(2,1)} async-done(((bf16[128,4,3696]{2,1,0:T(4,128)(2,1)}), bf16[128,4,3696]{2,1,0:T(4,128)(2,1)}, u32[]{:S(2)}, u32[]{:S(2)}) %all-to-all-start.2) | async-done | bytes 3784736 | tf_op jit(solution)/shard_map/all_to_all | solution.py:109
  351.3 7.0 %reshape.42 = bf16[512,3696]{1,0:T(8,128)(2,1)} reshape(bf16[128,4,3696]{2,1,0:T(4,128)(2,1)} %all-to-all-done.2) | data formatting | bytes 7569408 | tf_op jit(solution)/shard_map/reshape | solution.py:118
  358.3 6.0 %gather_fusion.1 = bf16[128,3696]{1,0:T(8,128)(2,1)} fusion(bf16[512,3696]{1,0:T(8,128)(2,1)} %reshape.42, s32[1024]{0:T(1024)S(1)} %pad_clamp_fusion), kind=kCustom, calls=%fused_computation.1 | custom fusion | bytes 1892864 | tf_op jit(solution)/shard_map/gather | solution.py:123
  364.3 29.1 %reduce-scatter.4.cloned.1.call-done = bf16[128,7392]{1,0:T(8,128)(2,1)} async-done(((bf16[2048,7392]{1,0:T(8,128)(2,1)}), bf16[128,7392]{1,0:T(8,128)(2,1)}) %reduce-scatter.4.cloned.1.call-update) | async-done | bytes 1892368 | tf_op jit(solution)/shard_map/reduce_scatter | solution.py:46
  (61 shorter events, 35.7 us)
Async XLA Ops:
  6.5 159.5 %copy-start = (bf16[1,8192,128]{2,1,0:T(8,128)(2,1)S(1)}, bf16[1,8192,128]{2,1,0:T(8,128)(2,1)}, u32[]{:S(2)}) copy-start(bf16[1,8192,128]{2,1,0:T(8,128)(2,1)} %param.10) | copy-start | bytes 6291460
  6.5 29.4 %copy-start.3 = (bf16[256,512]{1,0:T(8,128)(2,1)S(1)}, bf16[256,512]{1,0:T(8,128)(2,1)}, u32[]{:S(2)}) copy-start(bf16[256,512]{1,0:T(8,128)(2,1)} %param.7) | copy-start | bytes 786436
  6.5 386.9 %reduce-scatter.4.cloned.1.call-start = ((), (), s32[]{:S(2)}) async-start(), calls=%async_computation.4 | async-start | bytes 32309248 | tf_op jit(solution)/shard_map/reduce_scatter | solution.py:46
  6.5 6.3 %collective-permute-start = (bf16[256,512]{1,0:T(8,128)(2,1)}, bf16[256,512]{1,0:T(8,128)(2,1)S(1)}, u32[]{:S(2)}, u32[]{:S(2)}) collective-permute-start(bf16[256,512]{1,0:T(8,128)(2,1)} %param.7), channel_id=1, source_target_pairs={{0,1},{1,2},{2,3},{3,4},{4,5},{5,6},{6,7},{7,0},{8,9},{9,10},{10,1... | collective-permute-start | bytes 786440 | tf_op jit(solution)/shard_map/ppermute | solution.py:15
  12.9 5.7 %collective-permute-start.1 = (bf16[256,512]{1,0:T(8,128)(2,1)S(1)}, bf16[256,512]{1,0:T(8,128)(2,1)S(1)}, u32[]{:S(2)}, u32[]{:S(2)}) collective-permute-start(bf16[256,512]{1,0:T(8,128)(2,1)S(1)} %collective-permute-done), channel_id=1, source_target_pairs={{0,1},{1,2},{2,3},{3,4},{4,5},{5,6},{6,7},{7,0},{8,9},{9,10},{10,1... | collective-permute-start | bytes 786440 | tf_op jit(solution)/shard_map/ppermute | solution.py:15
  15.2 6.3 %collective-permute-start.4 = (bf16[256,512]{1,0:T(8,128)(2,1)}, bf16[256,512]{1,0:T(8,128)(2,1)S(1)}, u32[]{:S(2)}, u32[]{:S(2)}) collective-permute-start(bf16[256,512]{1,0:T(8,128)(2,1)} %param.7), channel_id=1, source_target_pairs={{0,7},{1,0},{2,1},{3,2},{4,3},{5,4},{6,5},{7,6},{8,15},{9,8},{10,9... | collective-permute-start | bytes 786440 | tf_op jit(solution)/shard_map/ppermute | solution.py:17
  18.6 5.8 %collective-permute-start.2 = (bf16[256,512]{1,0:T(8,128)(2,1)S(1)}, bf16[256,512]{1,0:T(8,128)(2,1)}, u32[]{:S(2)}, u32[]{:S(2)}) collective-permute-start(bf16[256,512]{1,0:T(8,128)(2,1)S(1)} %collective-permute-done.1), channel_id=1, source_target_pairs={{0,1},{1,2},{2,3},{3,4},{4,5},{5,6},{6,7},{7,0},{8,9},{9,10},{10,1... | collective-permute-start | bytes 786440 | tf_op jit(solution)/shard_map/ppermute | solution.py:15
  21.5 6.2 %collective-permute-start.5 = (bf16[256,512]{1,0:T(8,128)(2,1)S(1)}, bf16[256,512]{1,0:T(8,128)(2,1)S(1)}, u32[]{:S(2)}, u32[]{:S(2)}) collective-permute-start(bf16[256,512]{1,0:T(8,128)(2,1)S(1)} %collective-permute-done.4), channel_id=1, source_target_pairs={{0,7},{1,0},{2,1},{3,2},{4,3},{5,4},{6,5},{7,6},{8,15},{9,8},{10,9... | collective-permute-start | bytes 786440 | tf_op jit(solution)/shard_map/ppermute | solution.py:17
  24.4 6.3 %collective-permute-start.3 = (bf16[256,512]{1,0:T(8,128)(2,1)}, bf16[256,512]{1,0:T(8,128)(2,1)}, u32[]{:S(2)}, u32[]{:S(2)}) collective-permute-start(bf16[256,512]{1,0:T(8,128)(2,1)} %collective-permute-done.2), channel_id=1, source_target_pairs={{0,1},{1,2},{2,3},{3,4},{4,5},{5,6},{6,7},{7,0},{8,9},{9,10},{10,1... | collective-permute-start | bytes 786440 | tf_op jit(solution)/shard_map/ppermute | solution.py:15
  26.9 9.1 %copy-start.6 = (bf16[512,3696]{0,1:T(8,128)(2,1)S(1)}, bf16[512,3696]{0,1:T(8,128)(2,1)}, u32[]{:S(2)}) copy-start(bf16[512,3696]{0,1:T(8,128)(2,1)} %param.8) | copy-start | bytes 11354116
  27.7 6.2 %collective-permute-start.6 = (bf16[256,512]{1,0:T(8,128)(2,1)S(1)}, bf16[256,512]{1,0:T(8,128)(2,1)S(1)}, u32[]{:S(2)}, u32[]{:S(2)}) collective-permute-start(bf16[256,512]{1,0:T(8,128)(2,1)S(1)} %collective-permute-done.5), channel_id=1, source_target_pairs={{0,7},{1,0},{2,1},{3,2},{4,3},{5,4},{6,5},{7,6},{8,15},{9,8},{10,9... | collective-permute-start | bytes 786440 | tf_op jit(solution)/shard_map/ppermute | solution.py:17
  36.1 10.8 %copy-start.7 = (bf16[512,3696]{0,1:T(8,128)(2,1)S(1)}, bf16[512,3696]{0,1:T(8,128)(2,1)}, u32[]{:S(2)}) copy-start(bf16[512,3696]{0,1:T(8,128)(2,1)} %param.9) | copy-start | bytes 11354116
  115.6 0.7 copy-start.4
  115.6 0.7 copy-start.5
  122.6 43.4 %all-to-all-start = ((bf16[128,8,512]{2,1,0:T(8,128)(2,1)}), bf16[128,8,512]{2,1,0:T(8,128)(2,1)S(1)}, u32[]{:S(2)}, u32[]{:S(2)}) async-start(bf16[128,8,512]{2,1,0:T(8,128)(2,1)} %bitcast.46), calls=%async_computation | async-start | bytes 2097152 | tf_op jit(solution)/shard_map/all_to_all | solution.py:70
  175.4 87.1 %all-to-all-start.1 = ((bf16[128,4,3696]{2,1,0:T(4,128)(2,1)}), bf16[128,4,3696]{2,1,0:T(4,128)(2,1)}, u32[]{:S(2)}, u32[]{:S(2)}) async-start(bf16[128,4,3696]{2,1,0:T(4,128)(2,1)} %copy.52), calls=%async_computation.1 | async-start | bytes 7602176 | tf_op jit(solution)/shard_map/all_to_all | solution.py:102
  262.5 88.8 %all-to-all-start.2 = ((bf16[128,4,3696]{2,1,0:T(4,128)(2,1)}), bf16[128,4,3696]{2,1,0:T(4,128)(2,1)}, u32[]{:S(2)}, u32[]{:S(2)}) async-start(bf16[128,4,3696]{2,1,0:T(4,128)(2,1)} %copy.56), calls=%async_computation.2 | async-start | bytes 7602176 | tf_op jit(solution)/shard_map/all_to_all | solution.py:109
  393.4 1.9 copy-start.1
  393.4 2.0 copy-start.2
Sparse Core Ops, SparseCore 0:
  115.7 277.6 reduce-scatter.3
